TPU v7x, 256 devices: a whole 4x4x8 slice. The times are simulated.
256 devices in a mesh: section: 8 (over z), joint: 32 (over y, x, core).
Axes of the slice: x: 4, y: 4, z: 8, core: 2. Of those that a mesh axis runs over, the one named last changes fastest.
Arguments:
- encoder_rows: bfloat16 [32, 1024, 1536], P('joint', 'section'), may hold values from -6 to 6
- up_weight: bfloat16 [1536, 3072], P(None, 'section'), may hold values from -0.15625 to 0.15625
- down_weight: bfloat16 [3072, 1536], P('section'), may hold values from -0.109375 to 0.109375
- encoder_proj: bfloat16 [1536, 640], replicated, may hold values from -0.15625 to 0.15625
- embedding: bfloat16 [4096, 640], P('joint'), may hold values from -6 to 6
- conv_taps: float32 [2, 640], replicated, may hold values from -3 to 3
- decoder_proj: bfloat16 [640, 640], replicated, may hold values from -0.25 to 0.25
- output_proj: bfloat16 [640, 4096], replicated, may hold values from -0.5 to 0.5
- output_bias: float32 [4096], replicated, may hold values from -6 to 6
- frame_lengths: int32 [32], replicated, may hold values from 1 to 1024, 20480 in all
- label_lengths: int32 [32], replicated, may hold values from 1 to 3, 48 in all
- label_ids: int32 [32, 3], replicated, may hold values from 1 to 4095
- owner_index: int32 [32], replicated, may hold values from 0 to 31, each once
Outputs:
- enc_grad: bfloat16 [32, 1024, 1536], P('joint', 'section')
- up_grad: float32 [1536, 3072], P('joint', 'section')
- down_grad: float32 [3072, 1536], P('section', 'joint')
- pred_grad: float32 [32, 4, 640], P('joint', None, 'section')
Inputs may be any that keep to these rules, and one draw needn't show every extreme that they name: `owner_index`: every joint owner receives exactly one utterance. `frame_lengths`: the longest utterance uses all 1024 frames. `label_lengths`: the longest label sequence has 3 labels. `label_ids`: never the blank token 0.
All inputs are finite; a program needn't handle non-finite values.
Results may differ from a plain program's by a relative error of at most 0.013.
Values may be sent and summed in bfloat16 or wider, within the bound.
No kernel may reach another device: no remote copies, remote signals or barrier semaphores. Data moves between devices by JAX's collectives and lax.ppermute only.
A program may use at most 128 MiB of HBM per device.

v0:
```python
import jax
import jax.numpy as jnp
from jax import lax
from jax.sharding import PartitionSpec as P

NEG_BIG = -1000000000.0


def partner_2(block, axis, bit):
    count = lax.axis_size(axis)
    route = []
    for low in range(count):
        high = low | 1 << bit
        if high != low and high < count:
            route += [(low, high), (high, low)]
    return lax.ppermute(block, axis, route)


def from_behind(value, axis, steps):
    count = lax.axis_size(axis)
    initial, last = (max(0, -steps), min(count, count - steps))
    return lax.ppermute(value, axis, [(source, source + steps) for source in range(initial, last)])


def layer_norm(values):
    average = jnp.mean(values, axis=-1, keepdims=True)
    centered = values - average
    variance = jnp.mean(centered * centered, axis=-1, keepdims=True)
    inv_scale = lax.rsqrt(variance + 1e-05)
    return (centered * inv_scale, inv_scale)


def lower_paths(label_row):
    partial_sums = jnp.concatenate([jnp.zeros((1,), jnp.float32), jnp.cumsum(label_row)])
    places = partial_sums.shape[0]
    row_ids = lax.broadcasted_iota(jnp.int32, (places, places), 0)
    col_ids = lax.broadcasted_iota(jnp.int32, (places, places), 1)
    return jnp.where(col_ids <= row_ids, partial_sums[:, None] - partial_sums[None, :], NEG_BIG)


def advance(vector, blank_row, label_row, active):
    moved = blank_row + jax.nn.logsumexp(lower_paths(label_row) + vector[None, :], axis=1)
    return jnp.where(active, moved, vector)


def run_block(vector, blank_score, label_score, active):

    def run_one_frame(carried, inputs):
        blank_row, label_row, live_flag = inputs
        return (advance(carried, blank_row, label_row, live_flag), None)

    return lax.scan(run_one_frame, vector, (blank_score, label_score, active))[0]


def block_matrix(blank_score, label_score, active):
    places = blank_score.shape[1]
    row_ids = lax.broadcasted_iota(jnp.int32, (places, places), 0)
    col_ids = lax.broadcasted_iota(jnp.int32, (places, places), 1)
    identity_map = jnp.where(row_ids == col_ids, 0.0, NEG_BIG)

    def block_one_frame(carried, inputs):
        blank_row, label_row, live_flag = inputs
        moved = blank_row[:, None] + jax.nn.logsumexp(
            lower_paths(label_row)[:, :, None] + carried[None, :, :], axis=1
        )
        return (jnp.where(live_flag, moved, carried), None)

    return lax.scan(block_one_frame, identity_map, (blank_score, label_score, active))[0]


def log_apply(transfer, vector):
    return jax.nn.logsumexp(transfer + vector[None, :], axis=1)


def log_apply_back(transfer, vector):
    return jax.nn.logsumexp(transfer + vector[:, None], axis=0)


def joint_forward(frame_part, pred_here, label_row_ids, output_proj, output_bias):
    joined = jnp.tanh(frame_part.astype(jnp.float32)[:, None, :] + pred_here[None, :, :]).astype(
        jnp.bfloat16
    )
    frames_here, places, joint_width = joined.shape
    logits = (
        jnp.dot(
            joined.reshape(frames_here * places, joint_width),
            output_proj,
            preferred_element_type=jnp.float32,
        )
        + output_bias
    )
    logits = logits.reshape(frames_here, places, -1)
    exponent = jnp.exp(logits)
    denominator = jnp.sum(exponent, axis=-1, keepdims=True)
    log_total = jnp.log(denominator)[:, :, 0]
    blank_score = logits[:, :, 0] - log_total
    index_grid = jnp.broadcast_to(label_row_ids[None, :, None], (frames_here, places - 1, 1))
    picked = jnp.take_along_axis(logits[:, :-1, :], index_grid, axis=2)[:, :, 0]
    label_score = picked - log_total[:, :-1]
    posterior = exponent / denominator
    return (joined, posterior, blank_score, label_score)


def joint_backward(blank_grad, label_grad, label_row_ids, joined, posterior, output_proj):
    frames_here, places, vocab_size = posterior.shape
    label_full = jnp.pad(label_grad, ((0, 0), (0, 1)))
    weight_sum = blank_grad + label_full
    token_full = jnp.concatenate([label_row_ids, jnp.full((1,), -1, jnp.int32)])
    vocab_iota = lax.broadcasted_iota(jnp.int32, (1, 1, vocab_size), 2)
    blank_term = jnp.where(vocab_iota == 0, blank_grad[:, :, None], 0.0)
    label_term = jnp.where(vocab_iota == token_full[None, :, None], label_full[:, :, None], 0.0)
    logit_grad = -posterior * weight_sum[:, :, None] + blank_term + label_term
    logit_grad = logit_grad.astype(jnp.bfloat16).reshape(frames_here * places, vocab_size)
    joined_grad = lax.dot_general(
        logit_grad, output_proj, (((1,), (1,)), ((), ())), preferred_element_type=jnp.float32
    )
    joined_vals = joined.astype(jnp.float32).reshape(frames_here * places, -1)
    inner_grad = (joined_grad * (1.0 - joined_vals * joined_vals)).reshape(frames_here, places, -1)
    frame_part_grad = jnp.sum(inner_grad, axis=1).astype(jnp.bfloat16)
    pred_part_grad = jnp.sum(inner_grad, axis=0)
    return (frame_part_grad, pred_part_grad)


def network_sections(count):
    sections = []
    block_size = 2
    while block_size <= count:
        stride = block_size // 2
        while stride >= 1:
            sections.append((block_size, stride))
            stride = stride // 2
        block_size = block_size * 2
    return sections


def sort_section(keys, block_size, stride, device_id):
    count = keys.shape[0]
    position = jnp.arange(count, dtype=jnp.int32)
    partner = position ^ stride
    partner_keys = keys[partner]
    rising = position & block_size == 0
    lower_side = position < partner
    keep_small = lower_side == rising
    new_keys = jnp.where(
        keep_small, jnp.minimum(keys, partner_keys), jnp.maximum(keys, partner_keys)
    )
    takes = new_keys[device_id] != keys[device_id]
    return (new_keys, takes)


def route_owner(payload, keys, device_id, count):
    for block_size, stride in network_sections(count):
        keys, takes = sort_section(keys, block_size, stride, device_id)
        other = partner_2(payload, "joint", stride.bit_length() - 1)
        payload = jnp.where(takes, other, payload)
    return payload


def route_holder(payload, keys, device_id, count):
    for block_size, stride in network_sections(count):
        keys, takes = sort_section(keys, block_size, stride, device_id)
        other = partner_2(payload, "joint", stride.bit_length() - 1)
        payload = jnp.where(takes, other, payload)
    return payload


def on_device(
    encoder_rows,
    up_weight,
    down_weight,
    encoder_proj,
    embedding,
    conv_taps,
    decoder_proj,
    output_proj,
    output_bias,
    frame_lengths,
    label_lengths,
    label_ids,
    owner_index,
):
    section_count = lax.axis_size("section")
    joint_count = lax.axis_size("joint")
    section_id = lax.axis_index("section")
    joint_id = lax.axis_index("joint")
    block_len = encoder_rows.shape[1]
    utterances = label_ids.shape[0]
    places = label_ids.shape[1] + 1
    own_rows = encoder_rows[0].astype(jnp.float32)
    normed_in = layer_norm(own_rows)[0].astype(jnp.bfloat16)
    gathered = lax.all_gather(normed_in, "section", axis=0, tiled=True)
    pre_hidden = jnp.dot(gathered, up_weight, preferred_element_type=jnp.float32)
    hidden = jax.nn.silu(pre_hidden).astype(jnp.bfloat16)
    encoded = own_rows + lax.psum_scatter(
        0.5 * jnp.dot(hidden, down_weight, preferred_element_type=jnp.float32),
        "section",
        scatter_dimension=0,
        tiled=True,
    )
    unit_rows, inv_scale = layer_norm(encoded)
    frame_part = jnp.dot(
        unit_rows.astype(jnp.bfloat16), encoder_proj, preferred_element_type=jnp.float32
    ).astype(jnp.bfloat16)
    order_iota = jnp.arange(utterances, dtype=jnp.int32)
    inverse = jnp.zeros((utterances,), jnp.int32).at[owner_index].set(order_iota)
    own_utterance = inverse[joint_id]
    owner_frames = route_owner(frame_part, owner_index, joint_id, joint_count)
    context = jnp.concatenate([jnp.zeros((utterances, 1), jnp.int32), label_ids], axis=1)
    vocab_rows = embedding.shape[0]
    vocab_ids = joint_id * vocab_rows + jnp.arange(vocab_rows, dtype=jnp.int32)

    def label_term(start_row, row_count):
        number = row_count // places
        wanted = context[inverse].reshape(number * places)
        selector = (wanted[:, None] == vocab_ids[None, :]).astype(jnp.bfloat16)
        return jnp.dot(selector, embedding, preferred_element_type=jnp.float32)

    looked = lax.psum_scatter(
        label_term(jnp.int32(0), places * lax.axis_size("joint")).astype(jnp.bfloat16),
        "joint",
        scatter_dimension=0,
        tiled=True,
    ).astype(jnp.float32)
    previous = jnp.concatenate([looked[:1], looked[:-1]], axis=0)
    pred_act = jnp.maximum(conv_taps[0] * previous + conv_taps[1] * looked, 0.0).astype(
        jnp.bfloat16
    )
    pred_rows = jnp.dot(pred_act, decoder_proj, preferred_element_type=jnp.float32)
    label_here = label_ids[own_utterance]
    frames_used = frame_lengths[own_utterance]
    labels_used = label_lengths[own_utterance]
    joined, posterior, blank_score, label_score = joint_forward(
        owner_frames, pred_rows, label_here, output_proj, output_bias
    )
    frame_ids = section_id * block_len + jnp.arange(block_len, dtype=jnp.int32)
    active = frame_ids < frames_used
    transfer = block_matrix(blank_score, label_score, active)
    place_iota = jnp.arange(places, dtype=jnp.int32)
    start_vec = jnp.where(place_iota == 0, 0.0, NEG_BIG)
    finish_vec = jnp.where(place_iota == labels_used, 0.0, NEG_BIG)

    def forward_turn(turn_index, carried):
        passed = from_behind(log_apply(transfer, carried), "section", 1)
        return jnp.where(section_id == 0, start_vec, passed)

    incoming = lax.fori_loop(0, section_count - 1, forward_turn, start_vec)

    def backward_turn(turn_index, carried):
        passed = from_behind(log_apply_back(transfer, carried), "section", -1)
        return jnp.where(section_id == section_count - 1, finish_vec, passed)

    leaving = lax.fori_loop(0, section_count - 1, backward_turn, finish_vec)

    def block_out(blank_in, label_in):
        return run_block(incoming, blank_in, label_in, active)

    end_alpha, pullback = jax.vjp(block_out, blank_score, label_score)
    logprob = jax.nn.logsumexp(end_alpha + leaving)
    blank_grad, label_grad = pullback(-jnp.exp(end_alpha + leaving - logprob))
    frame_part_grad, pred_part = joint_backward(
        blank_grad, label_grad, label_here, joined, posterior, output_proj
    )
    part_grad = route_holder(frame_part_grad, inverse, joint_id, joint_count)
    unit_grad = lax.dot_general(
        part_grad, encoder_proj, (((1,), (1,)), ((), ())), preferred_element_type=jnp.float32
    )
    first_mean = jnp.mean(unit_grad, axis=-1, keepdims=True)
    second_mean = jnp.mean(unit_grad * unit_rows, axis=-1, keepdims=True)
    row_grad = (inv_scale * (unit_grad - first_mean - unit_rows * second_mean)).astype(jnp.bfloat16)
    grad_all = lax.all_gather(row_grad, "section", axis=0, tiled=True)
    hidden_grad = 0.5 * lax.dot_general(
        grad_all, down_weight, (((1,), (1,)), ((), ())), preferred_element_type=jnp.float32
    )
    gate_sigmoid = jax.nn.sigmoid(pre_hidden)
    pre_grad = (hidden_grad * gate_sigmoid * (1.0 + pre_hidden * (1.0 - gate_sigmoid))).astype(
        jnp.bfloat16
    )
    up_part = lax.dot_general(
        gathered, pre_grad, (((0,), (0,)), ((), ())), preferred_element_type=jnp.float32
    )
    down_part = 0.5 * lax.dot_general(
        hidden, grad_all, (((0,), (0,)), ((), ())), preferred_element_type=jnp.float32
    )
    up_sum, down_sum = (
        lax.psum_scatter(
            up_part.astype(jnp.bfloat16), "joint", scatter_dimension=0, tiled=True
        ).astype(jnp.float32),
        lax.psum_scatter(
            down_part.astype(jnp.bfloat16), "joint", scatter_dimension=1, tiled=True
        ).astype(jnp.float32),
    )
    pred_sum = lax.psum_scatter(pred_part[None], "section", scatter_dimension=2, tiled=True)
    return (row_grad[None], up_sum, down_sum, pred_sum)


def solution(mesh):
    return jax.shard_map(
        on_device,
        mesh=mesh,
        in_specs=(
            P("joint", "section", None),
            P(None, "section"),
            P("section", None),
            P(),
            P("joint", None),
            P(),
            P(),
            P(),
            P(),
            P(),
            P(),
            P(),
            P(),
        ),
        out_specs=(
            P("joint", "section", None),
            P("joint", "section"),
            P("section", "joint"),
            P("joint", None, "section"),
        ),
        check_vma=False,
    )
```

profile of v0, /device:TPU:2, one launch (start us, length us, event | category | flops | bytes accessed | tf_op | source)
XLA Modules:
  0.0 2108.3 jit_solution(6235568972007815648)
XLA Ops:
  12.7 48.0 %all-gather.3.cloned.1.call-done = bf16[1024,1536]{1,0:T(8,128)(2,1)} async-done(((bf16[128,1536]{1,0:T(8,128)(2,1)}), bf16[1024,1536]{1,0:T(8,128)(2,1)}) %all-gather.3.cloned.1.call-update) | async-done | bytes 3145744 | tf_op jit(solution)/shard_map/all_gather | solution.py:191
  65.7 4.5 convolution_multiply_fusion
  86.9 57.3 %reduce-scatter.7.cloned.1.call-done = f32[128,1536]{1,0:T(8,128)} async-done(((f32[1024,1536]{1,0:T(8,128)}), f32[128,1536]{1,0:T(8,128)}) %reduce-scatter.7.cloned.1.call-update) | async-done | bytes 786448 | tf_op jit(solution)/shard_map/reduce_scatter | solution.py:194
  179.8 5.0 collective-permute-done.8
  232.5 6.8 broadcast_in_dim.223
  246.4 9.4 exponential_reduce_fusion.3
  255.9 9.8 reshape.609
  266.7 5.5 gather_fusion.31
  275.0 308.2 %while.74 = (s32[]{:T(128)}, f32[4,4]{1,0:T(4,128)S(1)}, pred[128]{0:T(512)(128)(4,1)S(1)}, f32[128,4]{1,0:T(8,128)S(1)}, f32[128,3]{1,0:T(8,128)}, /*index=5*/s32[]{:T(128)}, f32[]{:T(128)}, f32[1]{0:T(128)}) while((s32[]{:T(128)}, f32[4,4]{1,0:T(4,128)S(1)}, pred[128]{0:T(512)(128)(4,1)S(1)}, f32[128,4]{1,0:T(8,128)S(1)}, ...), condition=%wide.region_12.13_spmd, body=%wide.region_8.0_spmd.sunk | while | flops 476 | bytes 1144 | solution.py:68
  583.2 39.8 %while.75 = (s32[]{:T(128)}, f32[4]{0:T(128)S(1)}, pred[]{:T(512)}, f32[4,4]{1,0:T(4,128)S(1)}, s32[]{:T(128)}) while((s32[]{:T(128)}, f32[4]{0:T(128)S(1)}, pred[]{:T(512)}, f32[4,4]{1,0:T(4,128)S(1)}, s32[]{:T(128)}) %tuple.157), condition=%wide.region_16.17_spmd.clone, body=%wide.region_13.16_spmd.clone.sunk | while | flops 110 | bytes 486 | solution.py:246
  610.0 4.7 collective-permute-start
  616.3 5.4 collective-permute-start
  623.0 567.5 %while.78 = (s32[]{:T(128)}, f32[4]{0:T(128)S(1)}, f32[128,4,4]{2,1,0:T(4,128)}, pred[128,4]{1,0:T(8,128)(4,1)}, f32[128,4]{1,0:T(8,128)S(1)}, /*index=5*/pred[1...) while((s32[]{:T(128)}, f32[4]{0:T(128)S(1)}, ...), condition=%wide.region_21.22_spmd.clone.clone, body=%wide.region_17.21_spmd.clone.clone.sunk | while | flops 296 | bytes 5132 | solution.py:52
  1190.5 53.7 %while.76 = (s32[]{:T(128)}, f32[4]{0:T(128)S(1)}, pred[]{:T(512)}, f32[4,4]{1,0:T(4,128)S(1)}, s32[]{:T(128)}, /*index=5*/s32[]{:T(128)}) while((s32[]{:T(128)}, f32[4]{0:T(128)S(1)}, pred[]{:T(512)}, f32[4,4]{1,0:T(4,128)S(1)}, s32[]{:T(128)}, /*index=5*/s32[]{:T(128)}) %tuple.183), condition=%wide.region_25.26_spmd.clone, body=%wide.region_22.25_spmd.clone.sunk | while | flops 110 | bytes 498 | solution.py:252
  1192.0 5.6 collective-permute-done.1
  1199.7 5.6 collective-permute-done.1
  1207.5 5.6 collective-permute-done.1
  1215.3 5.6 collective-permute-done.1
  1223.1 5.4 collective-permute-done.1
  1230.6 5.4 collective-permute-done.1
  1238.1 5.4 collective-permute-done.1
  1247.4 484.2 %while.77 = (s32[]{:T(128)}, f32[4]{0:T(128)S(1)}, f32[128,4]{1,0:T(8,128)S(1)}, f32[128,3]{1,0:T(8,128)S(1)}, pred[128]{0:T(512)(128)(4,1)S(1)}, /*index=5*/pre...) while((s32[]{:T(128)}, f32[4]{0:T(128)S(1)}, ...), condition=%wide.region_33.34_spmd.clone, body=%wide.region_28.33_spmd.clone.sunk | while | flops 133 | bytes 553 | solution.py:52
  1731.9 12.4 fusion.31
  1766.4 4.6 collective-permute-done.20
  1788.3 5.2 collective-permute-start.24
  1822.1 5.0 collective-permute-start.29
  1843.2 49.4 %all-gather.5.cloned.1.call-done = bf16[1024,1536]{1,0:T(8,128)(2,1)} async-done(((bf16[128,1536]{1,0:T(8,128)(2,1)}), bf16[1024,1536]{1,0:T(8,128)(2,1)}) %all-gather.5.cloned.1.call-update) | async-done | bytes 3145744 | tf_op jit(solution)/shard_map/all_gather | solution.py:270
  1892.6 5.3 fusion.30
  1898.0 7.8 convolution_convert_fusion
  1905.8 25.1 %reduce-scatter.13.cloned.1.call-done = f32[80,4]{1,0:T(8,128)} async-done(((f32[640,4]{1,0:T(8,128)}), f32[80,4]{1,0:T(8,128)}) %reduce-scatter.13.cloned.1.call-update) | async-done | bytes 1296
  1932.3 82.1 %reduce-scatter.11.cloned.1.call-done = bf16[384,48]{0,1:T(8,128)(2,1)} async-done(((bf16[384,1536]{0,1:T(8,128)(2,1)}), bf16[384,48]{0,1:T(8,128)(2,1)}) %reduce-scatter.11.cloned.1.call-update) | async-done | bytes 36880 | tf_op jit(solution)/shard_map/reduce_scatter | solution.py:288
  2015.8 83.2 %reduce-scatter.9.cloned.1.call-done = bf16[48,384]{1,0:T(8,128)(2,1)} async-done(((bf16[1536,384]{1,0:T(8,128)(2,1)}), bf16[48,384]{1,0:T(8,128)(2,1)}) %reduce-scatter.9.cloned.1.call-update) | async-done | bytes 36880 | tf_op jit(solution)/shard_map/reduce_scatter | solution.py:285
  (4265 shorter events, 1567.4 us)
Async XLA Ops:
  8.0 52.7 %all-gather.3.cloned.1.call-start = ((), (), s32[]{:S(2)}) async-start(), calls=%async_computation.4 | async-start | bytes 3538944 | tf_op jit(solution)/shard_map/all_gather | solution.py:191
  12.6 131.5 %reduce-scatter.7.cloned.1.call-start = ((), (), s32[]{:S(2)}) async-start(), calls=%async_computation.5 | async-start | bytes 7077888 | tf_op jit(solution)/shard_map/reduce_scatter | solution.py:194
  70.2 170.3 %all-reduce.5.cloned.1.call-start = ((), (), s32[]{:S(2)}) async-start(), calls=%async_computation.10 | async-start | bytes 327680
  74.8 1817.9 %all-gather.5.cloned.1.call-start = ((), (), s32[]{:S(2)}) async-start(), calls=%async_computation.6 | async-start | bytes 3538944 | tf_op jit(solution)/shard_map/all_gather | solution.py:270
  149.0 7.0 collective-permute-start.3
  160.2 7.8 collective-permute-start.5
  168.0 8.9 collective-permute-start.6
  178.4 6.4 collective-permute-start.8
  184.8 7.0 collective-permute-start.9
  191.9 6.3 collective-permute-start.10
  200.3 7.8 collective-permute-start.12
  213.7 6.9 collective-permute-start.14
  222.2 19.1 collective-permute-start.15
  610.0 6.0 collective-permute-start
  616.3 6.7 collective-permute-start
  1190.7 6.9 collective-permute-start.1
  1198.4 6.9 collective-permute-start.1
  1206.2 6.9 collective-permute-start.1
  1214.0 6.9 collective-permute-start.1
  1221.8 6.7 collective-permute-start.1
  1229.3 6.7 collective-permute-start.1
  1236.8 6.7 collective-permute-start.1
  1752.1 6.8 collective-permute-start.18
  1763.1 7.8 collective-permute-start.20
  1780.2 8.0 collective-permute-start.23
  1788.3 9.5 collective-permute-start.24
  1797.8 6.5 collective-permute-start.25
  1808.3 8.0 collective-permute-start.27
  1822.1 8.6 collective-permute-start.29
  1842.2 88.7 %reduce-scatter.13.cloned.1.call-start = ((), (), s32[]{:S(2)}) async-start(), calls=%async_computation.9 | async-start | bytes 368640
  1843.2 171.3 %reduce-scatter.11.cloned.1.call-start = ((), (), s32[]{:S(2)}) async-start(), calls=%async_computation.8 | async-start | bytes 1216512 | tf_op jit(solution)/shard_map/reduce_scatter | solution.py:288
  1897.9 201.1 %reduce-scatter.9.cloned.1.call-start = ((), (), s32[]{:S(2)}) async-start(), calls=%async_computation.7 | async-start | bytes 1216512 | tf_op jit(solution)/shard_map/reduce_scatter | solution.py:285
  (47 other events, 2084.4 us)
Sparse Core Ops, SparseCore 0:
  12.8 47.9 all-gather.2
  70.3 73.7 reduce-scatter.6
  1842.3 50.2 all-gather.4
  1895.0 35.8 reduce-scatter.12
  1934.6 79.7 reduce-scatter.10
  2018.1 80.8 reduce-scatter.8
Sparse Core Ops, SparseCore 1:
  74.9 107.8 all-reduce.4
where the time goes:
time: 2140 us; the launch traced here: 2110 us
  other arithmetic  813 us (38%)
  local copies, waits for them, and re-layouts  667 us (31%)
  waiting for transfers between devices  437 us (20%)
  starting transfers between devices  79.3 us (4%)
  between operations  60.3 us (3%)
  matrix products  46.8 us (2%)
    dynamic_slice x384, local copies, waits for them, and re-layouts, block_matrix(): lax.scan(block_one_frame, identity_map, (blank_score, label_score, active))  219 us
    another operation x386, local copies, waits for them, and re-layouts  187 us
    dynamic_update_slice x512, local copies, waits for them, and re-layouts, run_block(): lax.scan(run_one_frame, vector, (blank_score, label_score, active))[0]  173 us
    broadcast_in_dim x130, other arithmetic, run_block(): lax.scan(run_one_frame, vector, (blank_score, label_score, active))[0]  171 us
    reduce_sum x128, other arithmetic, lower_paths(): partial_sums[:, None] - partial_sums[None, :]  112 us
    dynamic_update_slice x128, other arithmetic, run_block(): lax.scan(run_one_frame, vector, (blank_score, label_score, active))[0]  84.6 us
    add_any x128, other arithmetic, advance(): vector[None, :]  84.1 us
    reduce_scatter x1, waiting for transfers between devices, on_device(): lax.psum_scatter(up_part.astype(jnp.bfloat16), 'joint', scatter_dimension...  83.2 us

commit v1 on v0

--- a/solution.py
+++ b/solution.py
@@ -2,6 +2,7 @@
 import jax.numpy as jnp
 from jax import lax
 from jax.sharding import PartitionSpec as P
+from jax.lax import axis_index, axis_size, ppermute
 
 NEG_BIG = -1000000000.0
 
@@ -188,7 +189,16 @@
     places = label_ids.shape[1] + 1
     own_rows = encoder_rows[0].astype(jnp.float32)
     normed_in = layer_norm(own_rows)[0].astype(jnp.bfloat16)
-    gathered = lax.all_gather(normed_in, "section", axis=0, tiled=True)
+    slots = axis_size("section")
+    all_blocks = [(kk, (kk + 1) % slots) for kk in range(slots)]
+    buffers = [(kk, (kk - 1) % slots) for kk in range(slots)]
+    spare, piece_now = ([normed_in], [normed_in])
+    for _ in range(slots // 2):
+        spare.append(ppermute(spare[-1], "section", all_blocks))
+    for _ in [*range((slots - 1) // 2)]:
+        piece_now.append(ppermute(piece_now[-1], "section", buffers))
+    met_up = jnp.concatenate([*spare[::-1], *piece_now[1:]], 0)
+    gathered = jnp.roll(met_up, (axis_index("section") - slots // 2) * normed_in.shape[0], 0)
     pre_hidden = jnp.dot(gathered, up_weight, preferred_element_type=jnp.float32)
     hidden = jax.nn.silu(pre_hidden).astype(jnp.bfloat16)
     encoded = own_rows + lax.psum_scatter(

time: 2140 us -> 2020 us (0.944)
  local copies, waits for them, and re-layouts: 667 us -> 538 us
  other arithmetic: 813 us -> 835 us
    another operation x386, local copies, waits for them, and re-layouts: 187 us -> 10.7 us
    all_gather x1 -> x0, waiting for transfers between devices: 48 us -> none  [on_device(): gathered = lax.all_gather(normed_in, 'section', axis=0, tiled=True)]
    dynamic_slice x384, local copies, waits for them, and re-layouts: 219 us -> 255 us  [block_matrix(): lax.scan(block_one_frame, identity_map, (blank_score, label_score, active))]
    ppermute x0 -> x7, waiting for transfers between devices: none -> 35.7 us  [the longest x4 35.7 us: on_device(): spare.append(ppermute(spare[-1], 'section', all_blocks))]
where the time goes in v1:
time: 2020 us; the launch traced here: 2000 us
  other arithmetic  835 us (41%)
  local copies, waits for them, and re-layouts  538 us (27%)
  waiting for transfers between devices  424 us (21%)
  starting transfers between devices  89.9 us (4%)
  between operations  60.1 us (3%)
  matrix products  45.3 us (2%)
    dynamic_slice x384, local copies, waits for them, and re-layouts, block_matrix(): lax.scan(block_one_frame, identity_map, (blank_score, label_score, active))  255 us
    dynamic_update_slice x512, local copies, waits for them, and re-layouts, run_block(): lax.scan(run_one_frame, vector, (blank_score, label_score, active))[0]  174 us
    broadcast_in_dim x130, other arithmetic, run_block(): lax.scan(run_one_frame, vector, (blank_score, label_score, active))[0]  168 us
    reduce_sum x128, other arithmetic, lower_paths(): partial_sums[:, None] - partial_sums[None, :]  112 us
    select_n x128, other arithmetic, block_one_frame(): return (jnp.where(live_flag, moved, carried), None)  96.9 us
    abs x128, other arithmetic, advance(): jax.nn.logsumexp(lower_paths(label_row) + vector[None, :], axis=1)  89.9 us
    dynamic_update_slice x128, other arithmetic, run_block(): lax.scan(run_one_frame, vector, (blank_score, label_score, active))[0]  84.6 us
    reduce_scatter x1, waiting for transfers between devices, on_device(): lax.psum_scatter(up_part.astype(jnp.bfloat16), 'joint', scatter_dimension...  83.1 us

profile of v1, /device:TPU:2, one launch (start us, length us, event | category | flops | bytes accessed | tf_op | source)
XLA Modules:
  0.0 1997.6 jit_solution(4881383716045071198)
XLA Ops:
  13.9 13.1 collective-permute-done.2
  30.2 8.3 collective-permute-done.3
  41.7 7.5 collective-permute-done.4
  52.4 6.9 collective-permute-done.5
  93.1 57.8 %reduce-scatter.7.cloned.1.call-done = f32[128,1536]{1,0:T(8,128)} async-done(((f32[1024,1536]{1,0:T(8,128)}), f32[128,1536]{1,0:T(8,128)}) %reduce-scatter.7.cloned.1.call-update) | async-done | bytes 786448 | tf_op jit(solution)/shard_map/reduce_scatter | solution.py:204
  185.1 4.8 collective-permute-done.15
  234.1 6.8 broadcast_in_dim.223
  245.8 9.4 exponential_reduce_fusion.3
  255.2 18.4 reshape.609
  274.6 5.5 gather_fusion.31
  280.8 252.4 %while.74 = (s32[]{:T(128)}, f32[4,4]{1,0:T(4,128)S(1)}, pred[128]{0:T(512)(128)(4,1)S(1)}, f32[128,4]{1,0:T(8,128)S(1)}, f32[128,3]{1,0:T(8,128)S(1)}, /*index=5*/s32[]{:T(128)}, f32[]{:T(128)}, f32[1]{0:T(128)}) while((s32[]{:T(128)}, f32[4,4]{1,0:T(4,128)S(1)}, pred[128]{0:T(512)(128)(4,1)S(1)}, f32[128,4]{1,0:T(8,128)S(1)}, ...), condition=%wide.region_12.13_spmd, body=%wide.region_8.12_spmd.sunk | while | flops 476 | bytes 1144 | solution.py:69
  533.2 39.8 %while.75 = (s32[]{:T(128)}, f32[4]{0:T(128)S(1)}, pred[]{:T(512)}, f32[4,4]{1,0:T(4,128)S(1)}, s32[]{:T(128)}) while((s32[]{:T(128)}, f32[4]{0:T(128)S(1)}, pred[]{:T(512)}, f32[4,4]{1,0:T(4,128)S(1)}, s32[]{:T(128)}) %tuple.158), condition=%wide.region_16.17_spmd.clone, body=%wide.region_13.16_spmd.clone.sunk | while | flops 110 | bytes 486 | solution.py:256
  560.1 4.7 collective-permute-start
  566.4 5.4 collective-permute-start
  573.1 511.7 %while.78 = (s32[]{:T(128)}, f32[4]{0:T(128)S(1)}, f32[128,4,4]{2,1,0:T(4,128)}, pred[128,4]{1,0:T(8,128)(4,1)}, f32[128,4]{1,0:T(8,128)S(1)}, /*index=5*/pred[1...) while((s32[]{:T(128)}, f32[4]{0:T(128)S(1)}, ...), condition=%wide.region_21.22_spmd.clone.clone, body=%wide.region_17.21_spmd.clone.clone.sunk | while | flops 296 | bytes 5132 | solution.py:53
  1084.7 53.6 %while.76 = (s32[]{:T(128)}, f32[4]{0:T(128)S(1)}, pred[]{:T(512)}, f32[4,4]{1,0:T(4,128)S(1)}, s32[]{:T(128)}, /*index=5*/s32[]{:T(128)}) while((s32[]{:T(128)}, f32[4]{0:T(128)S(1)}, pred[]{:T(512)}, f32[4,4]{1,0:T(4,128)S(1)}, s32[]{:T(128)}, /*index=5*/s32[]{:T(128)}) %tuple.182), condition=%wide.region_25.26_spmd.clone, body=%wide.region_22.25_spmd.clone.sunk | while | flops 110 | bytes 498 | solution.py:262
  1086.2 5.6 collective-permute-done.1
  1094.0 5.6 collective-permute-done.1
  1101.8 5.6 collective-permute-done.1
  1109.5 5.6 collective-permute-done.1
  1117.3 5.4 collective-permute-done.1
  1124.8 5.4 collective-permute-done.1
  1132.3 5.4 collective-permute-done.1
  1141.7 486.3 %while.77 = (s32[]{:T(128)}, f32[4]{0:T(128)S(1)}, f32[128,4]{1,0:T(8,128)S(1)}, f32[128,3]{1,0:T(8,128)S(1)}, pred[128]{0:T(512)(128)(4,1)S(1)}, /*index=5*/pre...) while((s32[]{:T(128)}, f32[4]{0:T(128)S(1)}, ...), condition=%wide.region_33.34_spmd.clone, body=%wide.region_28.33_spmd.clone.sunk | while | flops 133 | bytes 553 | solution.py:53
  1628.3 12.2 fusion.34
  1713.2 5.0 collective-permute-start.36
  1734.2 48.0 %all-gather.2.cloned.1.call-done = bf16[1024,1536]{1,0:T(8,128)(2,1)} async-done(((bf16[128,1536]{1,0:T(8,128)(2,1)}), bf16[1024,1536]{1,0:T(8,128)(2,1)}) %all-gather.2.cloned.1.call-update) | async-done | bytes 3145744 | tf_op jit(solution)/shard_map/all_gather | solution.py:280
  1782.1 5.3 fusion.30
  1787.8 7.8 convolution_convert_fusion
  1795.6 24.9 %reduce-scatter.13.cloned.1.call-done = f32[80,4]{1,0:T(8,128)} async-done(((f32[640,4]{1,0:T(8,128)}), f32[80,4]{1,0:T(8,128)}) %reduce-scatter.13.cloned.1.call-update) | async-done | bytes 1296
  1822.0 82.1 %reduce-scatter.11.cloned.1.call-done = bf16[384,48]{0,1:T(8,128)(2,1)} async-done(((bf16[384,1536]{0,1:T(8,128)(2,1)}), bf16[384,48]{0,1:T(8,128)(2,1)}) %reduce-scatter.11.cloned.1.call-update) | async-done | bytes 36880 | tf_op jit(solution)/shard_map/reduce_scatter | solution.py:298
  1905.5 83.1 %reduce-scatter.9.cloned.1.call-done = bf16[48,384]{1,0:T(8,128)(2,1)} async-done(((bf16[1536,384]{1,0:T(8,128)(2,1)}), bf16[48,384]{1,0:T(8,128)(2,1)}) %reduce-scatter.9.cloned.1.call-update) | async-done | bytes 36880 | tf_op jit(solution)/shard_map/reduce_scatter | solution.py:295
  (4305 shorter events, 1476.2 us)
Async XLA Ops:
  8.0 142.9 %reduce-scatter.7.cloned.1.call-start = ((), (), s32[]{:S(2)}) async-start(), calls=%async_computation.4 | async-start | bytes 7077888 | tf_op jit(solution)/shard_map/reduce_scatter | solution.py:204
  11.9 15.0 collective-permute-start.2
  26.9 11.5 collective-permute-start.3
  26.9 11.5 collective-permute-start.6
  38.4 10.7 collective-permute-start.4
  38.4 10.7 collective-permute-start.7
  49.2 10.1 collective-permute-start.5
  49.2 13.5 collective-permute-start.8
  76.5 165.7 %all-reduce.5.cloned.1.call-start = ((), (), s32[]{:S(2)}) async-start(), calls=%async_computation.9 | async-start | bytes 327680
  81.0 1701.1 %all-gather.2.cloned.1.call-start = ((), (), s32[]{:S(2)}) async-start(), calls=%async_computation.5 | async-start | bytes 3538944 | tf_op jit(solution)/shard_map/all_gather | solution.py:280
  157.1 7.1 collective-permute-start.10
  166.4 8.3 collective-permute-start.12
  174.7 7.3 collective-permute-start.13
  190.0 7.0 collective-permute-start.16
  204.0 7.8 collective-permute-start.19
  217.3 6.9 collective-permute-start.21
  224.3 18.6 collective-permute-start.22
  566.4 6.7 collective-permute-start
  1084.9 6.9 collective-permute-start.1
  1092.7 6.9 collective-permute-start.1
  1100.5 6.9 collective-permute-start.1
  1108.2 6.9 collective-permute-start.1
  1131.0 6.7 collective-permute-start.1
  1648.1 6.7 collective-permute-start.25
  1657.7 8.2 collective-permute-start.27
  1674.8 6.7 collective-permute-start.30
  1681.5 7.3 collective-permute-start.31
  1698.2 8.3 collective-permute-start.34
  1713.2 8.5 collective-permute-start.36
  1733.1 87.4 %reduce-scatter.13.cloned.1.call-start = ((), (), s32[]{:S(2)}) async-start(), calls=%async_computation.8 | async-start | bytes 368640
  1734.1 170.0 %reduce-scatter.11.cloned.1.call-start = ((), (), s32[]{:S(2)}) async-start(), calls=%async_computation.7 | async-start | bytes 1216512 | tf_op jit(solution)/shard_map/reduce_scatter | solution.py:298
  1787.5 201.2 %reduce-scatter.9.cloned.1.call-start = ((), (), s32[]{:S(2)}) async-start(), calls=%async_computation.6 | async-start | bytes 1216512 | tf_op jit(solution)/shard_map/reduce_scatter | solution.py:295
  (60 other events, 3897.1 us)
Sparse Core Ops, SparseCore 0:
  76.6 74.3 reduce-scatter.6
  1733.3 48.8 all-gather.1
  1784.7 35.8 reduce-scatter.12
  1824.3 79.7 reduce-scatter.10
  1907.8 80.8 reduce-scatter.8
Sparse Core Ops, SparseCore 1:
  81.1 108.4 all-reduce.4
